TPU v7x, 512 devices: a whole 4x8x8 slice. The times are simulated.
512 devices in a mesh: chan: 128 (over z, y, core), win: 4 (over x).
Axes of the slice: x: 4, y: 8, z: 8, core: 2. Of those that a mesh axis runs over, the one named last changes fastest.
Arguments:
- records: bfloat16 [16384, 16384], P('chan', 'win'), may hold values from -60 to 60
- offsets: int32 [4], replicated, may hold values from 1 to 15, as said below
- starts: int32 [4], P('win'), may hold values from 0 to 2048
Outputs:
- stacked: float32 [16, 4, 16384, 128], P('win', None, 'chan')
Inputs may be any that keep to these rules, and one draw needn't show every extreme that they name: The offsets are distinct, and the largest is 15.
All inputs are finite; a program needn't handle non-finite values.
Results may differ from a plain program's by a relative error of at most 0.006.
Values may be sent and summed in bfloat16 or wider, within the bound.
No kernel may reach another device: no remote copies, remote signals or barrier semaphores. Data moves between devices by JAX's collectives and lax.ppermute only.
A program may use at most 64 MiB of HBM per device.

v0:
```python
import math

import jax
import jax.numpy as jnp
import ml_dtypes
import numpy as np
from jax import lax
from jax.sharding import PartitionSpec as P

WIN = 2048
NBIN = 1024
BAND = 64
L = 16
K = 4
OFFCAP = 16


turn_full = 2.0 * math.pi


def dft_table():
    samples = np.arange(WIN, dtype=np.int64)
    bins = np.arange(NBIN, dtype=np.int64)
    turns = samples[:, None] * bins[None, :] % WIN
    angles = np.float32(turn_full / WIN) * turns.astype(np.float32)
    table = np.concatenate([np.cos(angles), -np.sin(angles)], axis=1)
    return jnp.asarray(table.astype(ml_dtypes.bfloat16))


def taper_weights():
    samples = jnp.arange(WIN, dtype=jnp.float32)
    return 0.5 - 0.5 * jnp.cos(turn_full / WIN * (samples + 0.5))


def band_matrix():
    bins = jnp.arange(NBIN, dtype=jnp.int32)
    near = (jnp.abs(bins[:, None] - bins[None, :]) <= BAND).astype(jnp.float32)
    return near / jnp.sum(near, axis=0, keepdims=True)


def phase_tables(windows_total):
    lags = jnp.arange(L, dtype=jnp.int32) - L // 2
    bins = jnp.arange(NBIN, dtype=jnp.int32)
    turns = bins[None, :] * (lags[:, None] + WIN) % WIN
    angles = turn_full / WIN * turns.astype(jnp.float32)
    weight = jnp.where(bins == 0, 1.0, 2.0).astype(jnp.float32) / (
        2.0 * math.sqrt(NBIN * windows_total)
    )
    return (jnp.cos(angles) * weight[None, :], jnp.sin(angles) * weight[None, :])


def whiten(frames, table, taper, band):
    values = frames.astype(jnp.float32)
    shaped = ((values - jnp.mean(values, axis=1, keepdims=True)) * taper[None, :]).astype(
        jnp.bfloat16
    )
    spec = jnp.dot(shaped, table, preferred_element_type=jnp.float32)
    real = spec[:, :NBIN]
    imag = spec[:, NBIN:]
    level = (
        jnp.dot(jnp.sqrt(real * real + imag * imag), band, precision=lax.Precision.HIGH) + 1e-05
    )
    return ((real / level).astype(jnp.bfloat16), (imag / level).astype(jnp.bfloat16))


def lag_factors(own_re, own_im, cos_w, sin_w):
    ar = own_re.astype(jnp.float32)[:, None, :]
    ai = own_im.astype(jnp.float32)[:, None, :]
    first = (ar * cos_w[None] - ai * sin_w[None]).astype(jnp.bfloat16)
    second = (ar * sin_w[None] + ai * cos_w[None]).astype(jnp.bfloat16)
    return first, second


def lag_terms(first, second, partner):
    return jnp.einsum(
        "ctf,kjf->tkcj", first, partner[:, 0], preferred_element_type=jnp.float32
    ) + jnp.einsum("ctf,kjf->tkcj", second, partner[:, 1], preferred_element_type=jnp.float32)


def split_for_win(corr):
    groups = lax.axis_size("win")
    return corr.reshape(groups, -1, *corr.shape[1:]).astype(jnp.bfloat16)


def pass_over_win(sent):
    return lax.all_to_all(sent, "win", split_axis=0, concat_axis=0, tiled=True)


def sum_over_win(arrived):
    return jnp.sum(arrived.astype(jnp.float32), axis=0)


def in_blocks(array, dim, size):
    before, after = (array.shape[:dim], array.shape[dim + 1 :])
    return jnp.moveaxis(array.reshape(*before, size, -1, *after), dim, 0)


def on_device(records, offsets, starts):
    n_chan = lax.axis_size("chan")
    groups = lax.axis_size("win")
    me = lax.axis_index("chan")
    frames = lax.dynamic_slice_in_dim(records, starts[0], WIN, 1)
    hops = jnp.minimum(offsets, OFFCAP - offsets)
    key = jnp.where(offsets == OFFCAP - 1, -1, hops * OFFCAP + offsets)
    order = jnp.sort(key)[1:] % OFFCAP
    rank = jnp.sum(key[None, :] < key[:, None], axis=1)
    frames, order, rank = lax.optimization_barrier((frames, order, rank))
    own_re, own_im = whiten(frames, dft_table(), taper_weights(), band_matrix())
    spectra = jnp.stack((own_re, own_im), axis=0)

    def shifted(by):
        pairs = [(i + by, i) for i in range(n_chan - by)]
        return lambda x: lax.ppermute(x, "chan", pairs)

    far = OFFCAP - 1
    farthest = shifted(far)(spectra)
    moves = [shifted(by) for by in range(1, far)]
    cos_w, sin_w = phase_tables(groups)
    first, second = lag_factors(own_re, own_im, cos_w, sin_w)
    nearer = [lax.switch(order[k] - 1, moves, spectra) for k in range(K - 2)]
    early = jnp.stack([farthest] + nearer, axis=0)
    early_sent = lax.optimization_barrier(split_for_win(lag_terms(first, second, early)))

    def with_early(move):
        return lambda x, sent: (move(x), pass_over_win(sent))

    last, early_arrived = lax.switch(
        order[K - 2] - 1, [with_early(move) for move in moves], spectra, early_sent
    )
    last_sent = split_for_win(lag_terms(first, second, last[None]))
    early_sum = sum_over_win(early_arrived)
    last_sum = sum_over_win(pass_over_win(last_sent))
    by_rank = jnp.concatenate([early_sum, last_sum], axis=1)
    return jnp.take(by_rank, rank, axis=1)


def solution(mesh):
    in_specs = (P("chan", "win"), P(), P("win"))
    out_specs = P("win", None, "chan", None)
    return jax.shard_map(
        on_device, mesh=mesh, in_specs=in_specs, out_specs=out_specs, check_vma=False
    )
```

profile of v0, /device:TPU:216, one launch (start us, length us, event | category | flops | bytes accessed | tf_op | source)
XLA Modules:
  0.0 132.1 jit_solution(1453649256275704610)
XLA Ops:
  0.1 0.2 convert_reduce_fusion.14
  1.0 0.7 compare_select_fusion.3
  1.8 0.7 sort.15
  2.6 0.2 constant_dynamic-slice_fusion
  3.0 4.7 %fusion.38 = f32[128,2048]{1,0:T(8,128)S(1)} fusion(bf16[2048,2048]{1,0:T(8,128)(2,1)} %constant.111.clone, bf16[128,2048]{1,0:T(8,128)(2,1)S(1)} %constant_dynamic-slice_fusion, f32[2048]{0:T(1024)S(1)} %multiply_subtract_fusion, f32[128]{0:T(128)S(1)} %broadcast_multiply_fusion), kind=kOutput, calls=%fused_computation.66 | convolution fusion | flops 1074790400 | bytes 9970176 | tf_op jit(solution)/shard_map/dot_general | solution.py:57
  7.7 1.2 fusion.52
  9.1 1.9 %collective-permute-start.42 = (bf16[2,128,1024]{2,1,0:T(8,128)(2,1)S(1)}, bf16[2,128,1024]{2,1,0:T(8,128)(2,1)S(1)}, u32[]{:S(2)}, u32[]{:S(2)}) collective-permute-start(bf16[2,128,1024]{2,1,0:T(8,128)(2,1)S(1)} %pad_maximum_fusion.2), channel_id=1, source_target_pairs={{60,0},{64,4},{68,8},{72,12},{76,16},{80,20},{84,24},{88,28},{92,3... | collective-permute-start | bytes 1572872 | tf_op jit(solution)/shard_map/ppermute | solution.py:113
  11.0 0.6 fusion.54
  12.8 28.8 %conditional.4 = (bf16[1,2,128,1024]{3,2,1,0:T(8,128)(2,1)}) conditional(s32[]{:T(128)} %bitcast.34, bf16[2,128,1024]{2,1,0:T(8,128)(2,1)S(1)} %pad_maximum_fusion.2, bf16[2,128,1024]{2,1,0:T(8,128)(2,1)S(1)} %pad_maximum_fusion.2, bf16[2,128,1024]{2,1,0:T(8,128)(2,1)S(1)} %pad_maximum_fusion.2, ...), branch_computations={%region_18.19_spmd, %region_19.20_spmd, %region_20.21_spmd, %regio... | conditional | bytes 2097200 | solution.py:120
  12.8 2.3 %collective-permute-start.17 = (bf16[2,128,1024]{2,1,0:T(8,128)(2,1)S(1)}, bf16[2,128,1024]{2,1,0:T(8,128)(2,1)}, u32[]{:S(2)}, u32[]{:S(2)}) collective-permute-start(bf16[2,128,1024]{2,1,0:T(8,128)(2,1)S(1)} %param.17), channel_id=1, source_target_pairs={{16,0},{20,4},{24,8},{28,12},{32,16},{36,20},{40,24},{44,28},{48,3... | collective-permute-start | bytes 1572872 | tf_op jit(solution)/shard_map/cond/branch_3_fun/ppermute | solution.py:113
  15.1 26.5 %collective-permute-done.17 = bf16[2,128,1024]{2,1,0:T(8,128)(2,1)} collective-permute-done((bf16[2,128,1024]{2,1,0:T(8,128)(2,1)S(1)}, bf16[2,128,1024]{2,1,0:T(8,128)(2,1)}, u32[]{:S(2)}, u32[]{:S(2)}) %collective-permute-start.17) | collective-permute-done | bytes 524320 | tf_op jit(solution)/shard_map/cond/branch_3_fun/ppermute | solution.py:113
  42.2 17.8 %conditional.3 = (bf16[1,2,128,1024]{3,2,1,0:T(8,128)(2,1)}) conditional(s32[]{:T(128)} %bitcast.33, bf16[2,128,1024]{2,1,0:T(8,128)(2,1)S(1)} %pad_maximum_fusion.2, bf16[2,128,1024]{2,1,0:T(8,128)(2,1)S(1)} %pad_maximum_fusion.2, bf16[2,128,1024]{2,1,0:T(8,128)(2,1)S(1)} %pad_maximum_fusion.2, ...), branch_computations={%region_4.5_spmd, %region_5.6_spmd, %region_6.7_spmd, %region_7.8_... | conditional | bytes 2097200 | solution.py:120
  42.2 2.4 %collective-permute-start.1 = (bf16[2,128,1024]{2,1,0:T(8,128)(2,1)S(1)}, bf16[2,128,1024]{2,1,0:T(8,128)(2,1)}, u32[]{:S(2)}, u32[]{:S(2)}) collective-permute-start(bf16[2,128,1024]{2,1,0:T(8,128)(2,1)S(1)} %param.1), channel_id=1, source_target_pairs={{8,0},{12,4},{16,8},{20,12},{24,16},{28,20},{32,24},{36,28},{40,32... | collective-permute-start | bytes 1572872 | tf_op jit(solution)/shard_map/cond/branch_1_fun/ppermute | solution.py:113
  44.6 15.4 %collective-permute-done.1 = bf16[2,128,1024]{2,1,0:T(8,128)(2,1)} collective-permute-done((bf16[2,128,1024]{2,1,0:T(8,128)(2,1)S(1)}, bf16[2,128,1024]{2,1,0:T(8,128)(2,1)}, u32[]{:S(2)}, u32[]{:S(2)}) %collective-permute-start.1) | collective-permute-done | bytes 524320 | tf_op jit(solution)/shard_map/cond/branch_1_fun/ppermute | solution.py:113
  60.1 0.3 cosine_multiply_fusion
  60.4 1.4 %pad_maximum_fusion = bf16[3,2,128,1024]{3,2,1,0:T(8,128)(2,1)S(1)} fusion(bf16[1,2,128,1024]{3,2,1,0:T(8,128)(2,1)} %get-tuple-element.315, bf16[1,2,128,1024]{3,2,1,0:T(8,128)(2,1)} %get-tuple-element.314, bf16[1,2,128,1024]{3,2,1,0:T(8,128)(2,1)S(1)} %bitcast.101), kind=kLoop, calls=%fused_computation.46 | loop fusion | flops 1572864 | bytes 3145728 | tf_op jit(solution)/shard_map/stack | solution.py:121
  61.8 1.9 %fusion.4 = f32[3,128,128,16]{2,1,3,0:T(8,128)S(1)} fusion(f32[16,1024]{1,0:T(8,128)S(1)} %get-tuple-element.282, f32[128,1024]{1,0:T(8,128)S(1)} %get-tuple-element.279, f32[16,1024]{1,0:T(8,128)S(1)} %get-tuple-element.281, f32[128,1024]{1,0:T(8,128)S(1)} %get-tuple-element.275, bf16[3,2,128,1024]{3,2,1,0:T(8,128)(2,1)S(1)} %pad_maximum_fusion), kind=kOutput, calls=%fused_computation.23 | convolution fusion | flops 1619001344 | bytes 5111808 | tf_op jit(solution)/shard_map/ctf,kjf->tkcj/dot_general | solution.py:77
  63.7 3.1 %add_convert_fusion.2 = bf16[3,128,128,16]{2,1,3,0:T(8,128)(2,1)S(1)} fusion(f32[3,128,128,16]{2,1,3,0:T(8,128)S(1)} %fusion.4, f32[16,1024]{1,0:T(8,128)S(1)} %get-tuple-element.282, f32[128,1024]{1,0:T(8,128)} %copy-done.5, f32[16,1024]{1,0:T(8,128)S(1)} %get-tuple-element.281, f32[128,1024]{1,0:T(8,128)} %copy-done.3, ...), kind=kOutput, calls=%fused_computation.43 | convolution fusion | flops 1620574208 | bytes 6684672 | tf_op jit(solution)/shard_map/ctf,kjf->tkcj/dot_general | solution.py:75
  66.8 40.8 %conditional.5 = (bf16[2,128,1024]{2,1,0:T(8,128)(2,1)}, f32[4,3,128,128]{3,2,1,0:T(8,128)S(1)}) conditional(s32[]{:T(128)} %bitcast.29, (bf16[2,128,1024]{2,1,0:T(8,128)(2,1)S(1)}, bf16[4,4,3,128,128]{3,4,1,0,2:T(8,128)(2,1)S(1)}) %tuple.295, (bf16[2,128,1024]{2,1,0:T(8,128)(2,1)S(1)}, ...), branch_computations={%region_32.34_spmd, %region_34.36_spmd, %region_36.38_spmd, %regio... | conditional | flops 1376256 | bytes 12320856 | solution.py:127
  67.0 1.6 %copy.62 = bf16[4,4,3,128,128]{4,3,2,1,0:T(8,128)(2,1)} copy(bf16[4,4,3,128,128]{3,4,1,0,2:T(8,128)(2,1)S(1)} %get-tuple-element.268) | data formatting | bytes 3145728 | tf_op jit(solution)/shard_map
  68.6 4.3 %all-to-all-start.10 = ((bf16[4,4,3,128,128]{4,3,2,1,0:T(8,128)(2,1)}), bf16[4,4,3,128,128]{4,3,2,1,0:T(8,128)(2,1)S(1)}, u32[]{:S(2)}, u32[]{:S(2)}) async-start(bf16[4,4,3,128,128]{4,3,2,1,0:T(8,128)(2,1)} %copy.62), calls=%async_computation.10 | async-start | bytes 3145728 | tf_op jit(solution)/shard_map/cond/branch_10_fun/all_to_all | solution.py:86
  72.9 1.9 %collective-permute-start.38 = (bf16[2,128,1024]{2,1,0:T(8,128)(2,1)S(1)}, bf16[2,128,1024]{2,1,0:T(8,128)(2,1)}, u32[]{:S(2)}, u32[]{:S(2)}) collective-permute-start(bf16[2,128,1024]{2,1,0:T(8,128)(2,1)S(1)} %get-tuple-element.143), channel_id=1, source_target_pairs={{44,0},{48,4},{52,8},{56,12},{60,16},{64,20},{68,24},{72,28},{76,3... | collective-permute-start | bytes 1572872 | tf_op jit(solution)/shard_map/cond/branch_10_fun/ppermute | solution.py:113
  74.8 19.1 %all-to-all-done.10 = bf16[4,4,3,128,128]{4,3,2,1,0:T(8,128)(2,1)S(1)} async-done(((bf16[4,4,3,128,128]{4,3,2,1,0:T(8,128)(2,1)}), bf16[4,4,3,128,128]{4,3,2,1,0:T(8,128)(2,1)S(1)}, u32[]{:S(2)}, u32[]{:S(2)}) %all-to-all-start.10) | async-done | bytes 1572896 | tf_op jit(solution)/shard_map/cond/branch_10_fun/all_to_all | solution.py:86
  93.9 0.3 convert_reduce_fusion.10
  94.2 13.4 %collective-permute-done.38 = bf16[2,128,1024]{2,1,0:T(8,128)(2,1)} collective-permute-done((bf16[2,128,1024]{2,1,0:T(8,128)(2,1)S(1)}, bf16[2,128,1024]{2,1,0:T(8,128)(2,1)}, u32[]{:S(2)}, u32[]{:S(2)}) %collective-permute-start.38) | collective-permute-done | bytes 524320 | tf_op jit(solution)/shard_map/cond/branch_10_fun/ppermute | solution.py:113
  107.6 3.1 %fusion = f32[128,128,16]{1,0,2:T(8,128)S(1)} fusion(f32[16,1024]{1,0:T(8,128)S(1)} %get-tuple-element.282, f32[128,1024]{1,0:T(8,128)} %copy-done.5, f32[16,1024]{1,0:T(8,128)S(1)} %get-tuple-element.281, f32[128,1024]{1,0:T(8,128)} %copy-done.3, bf16[1,2,128,1024]{3,2,1,0:T(8,128)(2,1)} %bitcast.45), kind=kOutput, calls=%fused_computation.19 | convolution fusion | flops 545259520 | bytes 2490368 | tf_op jit(solution)/shard_map/ctf,kjf->tkcj/dot_general | solution.py:75
  110.7 3.4 %fusion.30 = bf16[128,128,16]{1,0,2:T(8,128)(2,1)} fusion(f32[128,128,16]{1,0,2:T(8,128)S(1)} %fusion, f32[16,1024]{1,0:T(8,128)S(1)} %get-tuple-element.282, f32[128,1024]{1,0:T(8,128)S(1)} %copy-done.6, f32[16,1024]{1,0:T(8,128)S(1)} %get-tuple-element.281, f32[128,1024]{1,0:T(8,128)S(1)} %copy-done.4, bf16[1,2,128,1024]{3,2,1,0:T(8,128)(2,1)} %bitcast.45), kind=kOutput, calls=%fused_computation.50 | convolution fusion | flops 545783808 | bytes 3014656 | tf_op jit(solution)/shard_map/ctf,kjf->tkcj/dot_general | solution.py:77
  114.0 4.9 %all-to-all-start.14 = ((bf16[4,4,1,128,128]{3,4,1,2,0:T(8,128)(2,1)}), bf16[4,4,1,128,128]{3,4,1,2,0:T(8,128)(2,1)S(1)}, u32[]{:S(2)}, u32[]{:S(2)}) async-start(bf16[4,4,1,128,128]{3,4,1,2,0:T(8,128)(2,1)} %bitcast.53), calls=%async_computation.14 | async-start | bytes 1048576 | tf_op jit(solution)/shard_map/all_to_all | solution.py:86
  118.9 9.7 %all-to-all-done.14 = bf16[4,4,1,128,128]{3,4,1,2,0:T(8,128)(2,1)S(1)} async-done(((bf16[4,4,1,128,128]{3,4,1,2,0:T(8,128)(2,1)}), bf16[4,4,1,128,128]{3,4,1,2,0:T(8,128)(2,1)S(1)}, u32[]{:S(2)}, u32[]{:S(2)}) %all-to-all-start.14) | async-done | bytes 524320 | tf_op jit(solution)/shard_map/all_to_all | solution.py:86
  128.9 1.3 pad_maximum_fusion.1
  130.2 0.6 gather_fusion
  131.0 1.1 copy.69
  (30 shorter events, 1.0 us)
Async XLA Ops:
  0.0 2.6 %copy-start = (bf16[128,4096]{1,0:T(8,128)(2,1)S(1)}, bf16[128,4096]{1,0:T(8,128)(2,1)}, u32[]{:S(2)}) copy-start(bf16[128,4096]{1,0:T(8,128)(2,1)} %param.46) | copy-start | bytes 3145732
  9.0 52.8 %copy-start.3 = (f32[128,1024]{1,0:T(8,128)}, f32[128,1024]{1,0:T(8,128)S(1)}, u32[]{:S(2)}) copy-start(f32[128,1024]{1,0:T(8,128)S(1)} %get-tuple-element.275) | copy-start | bytes 1572868
  9.0 52.8 %copy-start.5 = (f32[128,1024]{1,0:T(8,128)}, f32[128,1024]{1,0:T(8,128)S(1)}, u32[]{:S(2)}) copy-start(f32[128,1024]{1,0:T(8,128)S(1)} %get-tuple-element.279) | copy-start | bytes 1572868
  9.1 51.3 %collective-permute-start.42 = (bf16[2,128,1024]{2,1,0:T(8,128)(2,1)S(1)}, bf16[2,128,1024]{2,1,0:T(8,128)(2,1)S(1)}, u32[]{:S(2)}, u32[]{:S(2)}) collective-permute-start(bf16[2,128,1024]{2,1,0:T(8,128)(2,1)S(1)} %pad_maximum_fusion.2), channel_id=1, source_target_pairs={{60,0},{64,4},{68,8},{72,12},{76,16},{80,20},{84,24},{88,28},{92,3... | collective-permute-start | bytes 1572872 | tf_op jit(solution)/shard_map/ppermute | solution.py:113
  12.8 28.7 %collective-permute-start.17 = (bf16[2,128,1024]{2,1,0:T(8,128)(2,1)S(1)}, bf16[2,128,1024]{2,1,0:T(8,128)(2,1)}, u32[]{:S(2)}, u32[]{:S(2)}) collective-permute-start(bf16[2,128,1024]{2,1,0:T(8,128)(2,1)S(1)} %param.17), channel_id=1, source_target_pairs={{16,0},{20,4},{24,8},{28,12},{32,16},{36,20},{40,24},{44,28},{48,3... | collective-permute-start | bytes 1572872 | tf_op jit(solution)/shard_map/cond/branch_3_fun/ppermute | solution.py:113
  42.2 17.8 %collective-permute-start.1 = (bf16[2,128,1024]{2,1,0:T(8,128)(2,1)S(1)}, bf16[2,128,1024]{2,1,0:T(8,128)(2,1)}, u32[]{:S(2)}, u32[]{:S(2)}) collective-permute-start(bf16[2,128,1024]{2,1,0:T(8,128)(2,1)S(1)} %param.1), channel_id=1, source_target_pairs={{8,0},{12,4},{16,8},{20,12},{24,16},{28,20},{32,24},{36,28},{40,32... | collective-permute-start | bytes 1572872 | tf_op jit(solution)/shard_map/cond/branch_1_fun/ppermute | solution.py:113
  68.6 25.3 %all-to-all-start.10 = ((bf16[4,4,3,128,128]{4,3,2,1,0:T(8,128)(2,1)}), bf16[4,4,3,128,128]{4,3,2,1,0:T(8,128)(2,1)S(1)}, u32[]{:S(2)}, u32[]{:S(2)}) async-start(bf16[4,4,3,128,128]{4,3,2,1,0:T(8,128)(2,1)} %copy.62), calls=%async_computation.10 | async-start | bytes 3145728 | tf_op jit(solution)/shard_map/cond/branch_10_fun/all_to_all | solution.py:86
  72.9 34.6 %collective-permute-start.38 = (bf16[2,128,1024]{2,1,0:T(8,128)(2,1)S(1)}, bf16[2,128,1024]{2,1,0:T(8,128)(2,1)}, u32[]{:S(2)}, u32[]{:S(2)}) collective-permute-start(bf16[2,128,1024]{2,1,0:T(8,128)(2,1)S(1)} %get-tuple-element.143), channel_id=1, source_target_pairs={{44,0},{48,4},{52,8},{56,12},{60,16},{64,20},{68,24},{72,28},{76,3... | collective-permute-start | bytes 1572872 | tf_op jit(solution)/shard_map/cond/branch_10_fun/ppermute | solution.py:113
  107.5 3.1 %copy-start.2 = (f32[4,3,128,128]{3,2,1,0:T(8,128)}, f32[4,3,128,128]{3,2,1,0:T(8,128)S(1)}, u32[]{:S(2)}) copy-start(f32[4,3,128,128]{3,2,1,0:T(8,128)S(1)} %get-tuple-element.161) | copy-start | bytes 2359300
  107.5 3.1 %copy-start.4 = (f32[128,1024]{1,0:T(8,128)S(1)}, f32[128,1024]{1,0:T(8,128)}, u32[]{:S(2)}) copy-start(f32[128,1024]{1,0:T(8,128)} %copy-done.3) | copy-start | bytes 1572868
  107.5 3.1 %copy-start.6 = (f32[128,1024]{1,0:T(8,128)S(1)}, f32[128,1024]{1,0:T(8,128)}, u32[]{:S(2)}) copy-start(f32[128,1024]{1,0:T(8,128)} %copy-done.5) | copy-start | bytes 1572868
  114.0 14.6 %all-to-all-start.14 = ((bf16[4,4,1,128,128]{3,4,1,2,0:T(8,128)(2,1)}), bf16[4,4,1,128,128]{3,4,1,2,0:T(8,128)(2,1)S(1)}, u32[]{:S(2)}, u32[]{:S(2)}) async-start(bf16[4,4,1,128,128]{3,4,1,2,0:T(8,128)(2,1)} %bitcast.53), calls=%async_computation.14 | async-start | bytes 1048576 | tf_op jit(solution)/shard_map/all_to_all | solution.py:86
  128.9 3.2 %copy-start.1 = (bf16[128,4096]{1,0:T(8,128)(2,1)S(1)}, bf16[128,4096]{1,0:T(8,128)(2,1)}, u32[]{:S(2)}) copy-start(bf16[128,4096]{1,0:T(8,128)(2,1)} %param.46) | copy-start | bytes 3145732
where the time goes:
time: 133 us; the launch traced here: 132 us
  waiting for transfers between devices  84.1 us (63%)
  starting transfers between devices  17.7 us (13%)
  matrix products  17.3 us (13%)
  other arithmetic  5.69 us (4%)
  local copies, waits for them, and re-layouts  4.26 us (3%)
  between operations  2.73 us (2%)
    ppermute x4, waiting for transfers between devices, shifted(): return lambda x: lax.ppermute(x, 'chan', pairs)  55.2 us
    all_to_all x2, waiting for transfers between devices, pass_over_win(): return lax.all_to_all(sent, 'win', split_axis=0, concat_axis=0, tiled=True)  28.8 us
    all_to_all x2, starting transfers between devices, pass_over_win(): return lax.all_to_all(sent, 'win', split_axis=0, concat_axis=0, tiled=True)  9.16 us
    ppermute x4, starting transfers between devices, shifted(): return lambda x: lax.ppermute(x, 'chan', pairs)  8.5 us
    dot_general x2, matrix products, lag_terms(): jnp.einsum('ctf,kjf->tkcj', first, partner[:, 0], preferred_element_type=...  6.15 us
    dot_general x2, matrix products, lag_terms(): jnp.einsum('ctf,kjf->tkcj', second, partner[:, 1], preferred_element_type...  5.23 us
    dot_general x1, matrix products, whiten(): spec = jnp.dot(shaped, table, preferred_element_type=jnp.float32)  4.69 us
  transfers between devices with their start and end apart: 6, of which 5 were waited for; matrix products, arithmetic and copies ran while one was open for 1% of the time, Pallas kernels for 0%

commit v1 on v0

--- a/solution.py
+++ b/solution.py
@@ -118,7 +118,7 @@
     cos_w, sin_w = phase_tables(groups)
     first, second = lag_factors(own_re, own_im, cos_w, sin_w)
     nearer = [lax.switch(order[k] - 1, moves, spectra) for k in range(K - 2)]
-    early = jnp.stack([farthest] + nearer, axis=0)
+    early = jnp.stack(nearer, axis=0)
     early_sent = lax.optimization_barrier(split_for_win(lag_terms(first, second, early)))
 
     def with_early(move):
@@ -127,10 +127,10 @@
     last, early_arrived = lax.switch(
         order[K - 2] - 1, [with_early(move) for move in moves], spectra, early_sent
     )
-    last_sent = split_for_win(lag_terms(first, second, last[None]))
+    last_sent = split_for_win(lag_terms(first, second, jnp.stack([last, farthest], axis=0)))
     early_sum = sum_over_win(early_arrived)
     last_sum = sum_over_win(pass_over_win(last_sent))
-    by_rank = jnp.concatenate([early_sum, last_sum], axis=1)
+    by_rank = jnp.concatenate([last_sum[:, 1:], early_sum, last_sum[:, :1]], axis=1)
     return jnp.take(by_rank, rank, axis=1)
 
 

time: 133 us -> 169 us (1.27)
  the two profiles are of different devices: /device:TPU:216 before, /device:TPU:240 now
where the time goes in v1:
time: 169 us; the launch traced here: 168 us
  waiting for transfers between devices  120 us (71%)
  starting transfers between devices  18.5 us (11%)
  matrix products  16.2 us (10%)
  local copies, waits for them, and re-layouts  5.26 us (3%)
  other arithmetic  5 us (3%)
  between operations  2.81 us (2%)
    ppermute x4, waiting for transfers between devices, shifted(): return lambda x: lax.ppermute(x, 'chan', pairs)  92.4 us
    all_to_all x2, waiting for transfers between devices, pass_over_win(): return lax.all_to_all(sent, 'win', split_axis=0, concat_axis=0, tiled=True)  27.6 us
    ppermute x4, starting transfers between devices, shifted(): return lambda x: lax.ppermute(x, 'chan', pairs)  9.67 us
    all_to_all x2, starting transfers between devices, pass_over_win(): return lax.all_to_all(sent, 'win', split_axis=0, concat_axis=0, tiled=True)  8.83 us
    dot_general x2, matrix products, lag_terms(): jnp.einsum('ctf,kjf->tkcj', first, partner[:, 0], preferred_element_type=...  5.5 us
    dot_general x2, matrix products, lag_terms(): jnp.einsum('ctf,kjf->tkcj', second, partner[:, 1], preferred_element_type...  4.79 us
    dot_general x1, matrix products, whiten(): spec = jnp.dot(shaped, table, preferred_element_type=jnp.float32)  4.69 us
  transfers between devices with their start and end apart: 6, of which 5 were waited for; matrix products, arithmetic and copies ran while one was open for 4% of the time, Pallas kernels for 0%

profile of v1, /device:TPU:240, one launch (start us, length us, event | category | flops | bytes accessed | tf_op | source)
XLA Modules:
  0.0 168.1 jit_solution(17029042180973152575)
XLA Ops:
  0.1 0.2 convert_reduce_fusion.14
  1.0 0.7 compare_select_fusion.3
  1.8 0.7 sort.15
  2.6 0.2 constant_dynamic-slice_fusion
  3.0 4.7 %fusion.36 = f32[128,2048]{1,0:T(8,128)S(1)} fusion(bf16[2048,2048]{1,0:T(8,128)(2,1)} %constant.111.clone, bf16[128,2048]{1,0:T(8,128)(2,1)S(1)} %constant_dynamic-slice_fusion, f32[2048]{0:T(1024)S(1)} %multiply_subtract_fusion, f32[128]{0:T(128)S(1)} %broadcast_multiply_fusion), kind=kOutput, calls=%fused_computation.60 | convolution fusion | flops 1074790400 | bytes 9970176 | tf_op jit(solution)/shard_map/dot_general | solution.py:57
  7.7 1.2 fusion.54
  9.0 0.9 pad_maximum_fusion.3
  9.9 1.9 %collective-permute-start.42 = (bf16[2,128,1024]{2,1,0:T(8,128)(2,1)}, bf16[2,128,1024]{2,1,0:T(8,128)(2,1)S(1)}, u32[]{:S(2)}, u32[]{:S(2)}) collective-permute-start(bf16[2,128,1024]{2,1,0:T(8,128)(2,1)} %pad_maximum_fusion.3), channel_id=1, source_target_pairs={{60,0},{64,4},{68,8},{72,12},{76,16},{80,20},{84,24},{88,28},{92,3... | collective-permute-start | bytes 1572872 | tf_op jit(solution)/shard_map/ppermute | solution.py:113
  11.9 0.6 fusion.57
  13.2 43.6 %conditional.4 = (bf16[1,2,128,1024]{3,2,1,0:T(8,128)(2,1)}) conditional(s32[]{:T(128)} %bitcast.48, bf16[2,128,1024]{2,1,0:T(8,128)(2,1)} %pad_maximum_fusion.3, bf16[2,128,1024]{2,1,0:T(8,128)(2,1)} %pad_maximum_fusion.3, bf16[2,128,1024]{2,1,0:T(8,128)(2,1)} %pad_maximum_fusion.3, ...), branch_computations={%region_18.19_spmd, %region_19.20_spmd, %region_20.21_spmd, %regio... | conditional | bytes 2097200 | solution.py:120
  13.2 3.9 %collective-permute-start.19 = (bf16[2,128,1024]{2,1,0:T(8,128)(2,1)}, bf16[2,128,1024]{2,1,0:T(8,128)(2,1)}, u32[]{:S(2)}, u32[]{:S(2)}) collective-permute-start(bf16[2,128,1024]{2,1,0:T(8,128)(2,1)} %param.19), channel_id=1, source_target_pairs={{24,0},{28,4},{32,8},{36,12},{40,16},{44,20},{48,24},{52,28},{56,3... | collective-permute-start | bytes 1572872 | tf_op jit(solution)/shard_map/cond/branch_5_fun/ppermute | solution.py:113
  17.2 39.6 %collective-permute-done.19 = bf16[2,128,1024]{2,1,0:T(8,128)(2,1)} collective-permute-done((bf16[2,128,1024]{2,1,0:T(8,128)(2,1)}, bf16[2,128,1024]{2,1,0:T(8,128)(2,1)}, u32[]{:S(2)}, u32[]{:S(2)}) %collective-permute-start.19) | collective-permute-done | bytes 524320 | tf_op jit(solution)/shard_map/cond/branch_5_fun/ppermute | solution.py:113
  57.4 31.4 %conditional.3 = (bf16[1,2,128,1024]{3,2,1,0:T(8,128)(2,1)}) conditional(s32[]{:T(128)} %bitcast.46, bf16[2,128,1024]{2,1,0:T(8,128)(2,1)} %pad_maximum_fusion.3, bf16[2,128,1024]{2,1,0:T(8,128)(2,1)} %pad_maximum_fusion.3, bf16[2,128,1024]{2,1,0:T(8,128)(2,1)} %pad_maximum_fusion.3, ...), branch_computations={%region_4.5_spmd, %region_5.6_spmd, %region_6.7_spmd, %region_7.8_... | conditional | bytes 2097200 | solution.py:120
  57.5 1.9 %collective-permute-start.3 = (bf16[2,128,1024]{2,1,0:T(8,128)(2,1)}, bf16[2,128,1024]{2,1,0:T(8,128)(2,1)}, u32[]{:S(2)}, u32[]{:S(2)}) collective-permute-start(bf16[2,128,1024]{2,1,0:T(8,128)(2,1)} %param.3), channel_id=1, source_target_pairs={{16,0},{20,4},{24,8},{28,12},{32,16},{36,20},{40,24},{44,28},{48,3... | collective-permute-start | bytes 1572872 | tf_op jit(solution)/shard_map/cond/branch_3_fun/ppermute | solution.py:113
  59.4 29.5 %collective-permute-done.3 = bf16[2,128,1024]{2,1,0:T(8,128)(2,1)} collective-permute-done((bf16[2,128,1024]{2,1,0:T(8,128)(2,1)}, bf16[2,128,1024]{2,1,0:T(8,128)(2,1)}, u32[]{:S(2)}, u32[]{:S(2)}) %collective-permute-start.3) | collective-permute-done | bytes 524320 | tf_op jit(solution)/shard_map/cond/branch_3_fun/ppermute | solution.py:113
  88.9 0.3 cosine_multiply_fusion
  89.2 2.4 %fusion.5 = f32[2,128,128,16]{2,1,3,0:T(8,128)S(1)} fusion(f32[16,1024]{1,0:T(8,128)S(1)} %get-tuple-element.285, f32[128,1024]{1,0:T(8,128)S(1)} %get-tuple-element.280, f32[16,1024]{1,0:T(8,128)S(1)} %get-tuple-element.284, f32[128,1024]{1,0:T(8,128)S(1)} %get-tuple-element.276, bf16[1,2,128,1024]{3,2,0,1:T(8,128)(2,1)} %bitcast.49, ...), kind=kOutput, calls=%fused_computation.24 | convolution fusion | flops 1083179008 | bytes 4325376 | tf_op jit(solution)/shard_map/ctf,kjf->tkcj/dot_general | solution.py:77
  92.2 2.7 %add_convert_fusion.2 = bf16[2,128,128,16]{2,1,3,0:T(8,128)(2,1)S(1)} fusion(f32[2,128,128,16]{2,1,3,0:T(8,128)S(1)} %fusion.5, f32[16,1024]{1,0:T(8,128)S(1)} %get-tuple-element.285, f32[128,1024]{1,0:T(8,128)} %copy-done.4, f32[16,1024]{1,0:T(8,128)S(1)} %get-tuple-element.284, f32[128,1024]{1,0:T(8,128)S(1)} %get-tuple-element.276, ...), kind=kOutput, calls=%fused_computation.29 | convolution fusion | flops 1084227584 | bytes 5373952 | tf_op jit(solution)/shard_map/ctf,kjf->tkcj/dot_general | solution.py:75
  94.9 43.7 %conditional.5 = (bf16[1,2,128,1024]{3,2,1,0:T(8,128)(2,1)}, f32[4,2,128,128]{3,2,1,0:T(8,128)S(1)}) conditional(s32[]{:T(128)} %bitcast.43, (bf16[2,128,1024]{2,1,0:T(8,128)(2,1)}, bf16[4,4,2,128,128]{3,4,1,0,2:T(8,128)(2,1)S(1)}) %tuple.310, (bf16[2,128,1024]{2,1,0:T(8,128)(2,1)}, ...), branch_computations={%region_32.34_spmd, %region_34.36_spmd, %region_36.38_spmd, %regio... | conditional | flops 917504 | bytes 8912984 | solution.py:127
  95.1 1.3 copy.70
  96.4 4.3 %all-to-all-start.9 = ((bf16[4,4,2,128,128]{4,3,2,1,0:T(8,128)(2,1)}), bf16[4,4,2,128,128]{4,3,2,1,0:T(8,128)(2,1)S(1)}, u32[]{:S(2)}, u32[]{:S(2)}) async-start(bf16[4,4,2,128,128]{4,3,2,1,0:T(8,128)(2,1)} %copy.70), calls=%async_computation.9 | async-start | bytes 2097152 | tf_op jit(solution)/shard_map/cond/branch_9_fun/all_to_all | solution.py:86
  100.7 1.9 %collective-permute-start.37 = (bf16[2,128,1024]{2,1,0:T(8,128)(2,1)}, bf16[2,128,1024]{2,1,0:T(8,128)(2,1)}, u32[]{:S(2)}, u32[]{:S(2)}) collective-permute-start(bf16[2,128,1024]{2,1,0:T(8,128)(2,1)} %get-tuple-element.142), channel_id=1, source_target_pairs={{40,0},{44,4},{48,8},{52,12},{56,16},{60,20},{64,24},{68,28},{72,3... | collective-permute-start | bytes 1572872 | tf_op jit(solution)/shard_map/cond/branch_9_fun/ppermute | solution.py:113
  102.7 12.5 %all-to-all-done.9 = bf16[4,4,2,128,128]{4,3,2,1,0:T(8,128)(2,1)S(1)} async-done(((bf16[4,4,2,128,128]{4,3,2,1,0:T(8,128)(2,1)}), bf16[4,4,2,128,128]{4,3,2,1,0:T(8,128)(2,1)S(1)}, u32[]{:S(2)}, u32[]{:S(2)}) %all-to-all-start.9) | async-done | bytes 1048608 | tf_op jit(solution)/shard_map/cond/branch_9_fun/all_to_all | solution.py:86
  115.3 23.3 %collective-permute-done.37 = bf16[2,128,1024]{2,1,0:T(8,128)(2,1)} collective-permute-done((bf16[2,128,1024]{2,1,0:T(8,128)(2,1)}, bf16[2,128,1024]{2,1,0:T(8,128)(2,1)}, u32[]{:S(2)}, u32[]{:S(2)}) %collective-permute-start.37) | collective-permute-done | bytes 524320 | tf_op jit(solution)/shard_map/cond/branch_9_fun/ppermute | solution.py:113
  138.6 2.8 %fusion.7 = f32[2,128,128,16]{2,1,3,0:T(8,128)S(1)} fusion(f32[16,1024]{1,0:T(8,128)S(1)} %get-tuple-element.285, f32[128,1024]{1,0:T(8,128)} %copy-done.4, f32[16,1024]{1,0:T(8,128)S(1)} %get-tuple-element.284, f32[128,1024]{1,0:T(8,128)} %copy-done.2, bf16[1,2,128,1024]{3,2,1,0:T(8,128)(2,1)} %get-tuple-element.162, ...), kind=kOutput, calls=%fused_computation.25 | convolution fusion | flops 1083179008 | bytes 4325376 | tf_op jit(solution)/shard_map/ctf,kjf->tkcj/dot_general | solution.py:75
  141.5 2.4 %add_convert_fusion.1 = bf16[2,128,128,16]{2,1,3,0:T(8,128)(2,1)S(1)} fusion(f32[2,128,128,16]{2,1,3,0:T(8,128)S(1)} %fusion.7, f32[16,1024]{1,0:T(8,128)S(1)} %get-tuple-element.285, f32[128,1024]{1,0:T(8,128)S(1)} %copy-done.5, f32[16,1024]{1,0:T(8,128)S(1)} %get-tuple-element.284, f32[128,1024]{1,0:T(8,128)S(1)} %copy-done.3, ...), kind=kOutput, calls=%fused_computation.28 | convolution fusion | flops 1084227584 | bytes 5373952 | tf_op jit(solution)/shard_map/ctf,kjf->tkcj/dot_general | solution.py:77
  143.9 1.1 copy.75
  145.0 4.5 %all-to-all-start.14 = ((bf16[4,4,2,128,128]{3,4,1,2,0:T(8,128)(2,1)}), bf16[4,4,2,128,128]{3,4,1,2,0:T(8,128)(2,1)S(1)}, u32[]{:S(2)}, u32[]{:S(2)}) async-start(bf16[4,4,2,128,128]{3,4,1,2,0:T(8,128)(2,1)} %copy.75), calls=%async_computation.14 | async-start | bytes 2097152 | tf_op jit(solution)/shard_map/all_to_all | solution.py:86
  149.5 15.1 %all-to-all-done.14 = bf16[4,4,2,128,128]{3,4,1,2,0:T(8,128)(2,1)S(1)} async-done(((bf16[4,4,2,128,128]{3,4,1,2,0:T(8,128)(2,1)}), bf16[4,4,2,128,128]{3,4,1,2,0:T(8,128)(2,1)S(1)}, u32[]{:S(2)}, u32[]{:S(2)}) %all-to-all-start.14) | async-done | bytes 1048608 | tf_op jit(solution)/shard_map/all_to_all | solution.py:86
  165.1 1.1 pad_maximum_fusion
  166.3 0.6 gather_fusion
  167.1 1.1 copy.79
  (30 shorter events, 1.3 us)
Async XLA Ops:
  0.0 2.6 %copy-start = (bf16[128,4096]{1,0:T(8,128)(2,1)S(1)}, bf16[128,4096]{1,0:T(8,128)(2,1)}, u32[]{:S(2)}) copy-start(bf16[128,4096]{1,0:T(8,128)(2,1)} %param.46) | copy-start | bytes 3145732
  9.0 83.2 %copy-start.4 = (f32[128,1024]{1,0:T(8,128)}, f32[128,1024]{1,0:T(8,128)S(1)}, u32[]{:S(2)}) copy-start(f32[128,1024]{1,0:T(8,128)S(1)} %get-tuple-element.280) | copy-start | bytes 1572868
  9.0 85.9 %copy-start.2 = (f32[128,1024]{1,0:T(8,128)}, f32[128,1024]{1,0:T(8,128)S(1)}, u32[]{:S(2)}) copy-start(f32[128,1024]{1,0:T(8,128)S(1)} %get-tuple-element.276) | copy-start | bytes 1572868
  9.9 128.7 %collective-permute-start.42 = (bf16[2,128,1024]{2,1,0:T(8,128)(2,1)}, bf16[2,128,1024]{2,1,0:T(8,128)(2,1)S(1)}, u32[]{:S(2)}, u32[]{:S(2)}) collective-permute-start(bf16[2,128,1024]{2,1,0:T(8,128)(2,1)} %pad_maximum_fusion.3), channel_id=1, source_target_pairs={{60,0},{64,4},{68,8},{72,12},{76,16},{80,20},{84,24},{88,28},{92,3... | collective-permute-start | bytes 1572872 | tf_op jit(solution)/shard_map/ppermute | solution.py:113
  13.2 43.6 %collective-permute-start.19 = (bf16[2,128,1024]{2,1,0:T(8,128)(2,1)}, bf16[2,128,1024]{2,1,0:T(8,128)(2,1)}, u32[]{:S(2)}, u32[]{:S(2)}) collective-permute-start(bf16[2,128,1024]{2,1,0:T(8,128)(2,1)} %param.19), channel_id=1, source_target_pairs={{24,0},{28,4},{32,8},{36,12},{40,16},{44,20},{48,24},{52,28},{56,3... | collective-permute-start | bytes 1572872 | tf_op jit(solution)/shard_map/cond/branch_5_fun/ppermute | solution.py:113
  57.5 31.4 %collective-permute-start.3 = (bf16[2,128,1024]{2,1,0:T(8,128)(2,1)}, bf16[2,128,1024]{2,1,0:T(8,128)(2,1)}, u32[]{:S(2)}, u32[]{:S(2)}) collective-permute-start(bf16[2,128,1024]{2,1,0:T(8,128)(2,1)} %param.3), channel_id=1, source_target_pairs={{16,0},{20,4},{24,8},{28,12},{32,16},{36,20},{40,24},{44,28},{48,3... | collective-permute-start | bytes 1572872 | tf_op jit(solution)/shard_map/cond/branch_3_fun/ppermute | solution.py:113
  96.4 18.7 %all-to-all-start.9 = ((bf16[4,4,2,128,128]{4,3,2,1,0:T(8,128)(2,1)}), bf16[4,4,2,128,128]{4,3,2,1,0:T(8,128)(2,1)S(1)}, u32[]{:S(2)}, u32[]{:S(2)}) async-start(bf16[4,4,2,128,128]{4,3,2,1,0:T(8,128)(2,1)} %copy.70), calls=%async_computation.9 | async-start | bytes 2097152 | tf_op jit(solution)/shard_map/cond/branch_9_fun/all_to_all | solution.py:86
  100.7 37.9 %collective-permute-start.37 = (bf16[2,128,1024]{2,1,0:T(8,128)(2,1)}, bf16[2,128,1024]{2,1,0:T(8,128)(2,1)}, u32[]{:S(2)}, u32[]{:S(2)}) collective-permute-start(bf16[2,128,1024]{2,1,0:T(8,128)(2,1)} %get-tuple-element.142), channel_id=1, source_target_pairs={{40,0},{44,4},{48,8},{52,12},{56,16},{60,20},{64,24},{68,28},{72,3... | collective-permute-start | bytes 1572872 | tf_op jit(solution)/shard_map/cond/branch_9_fun/ppermute | solution.py:113
  138.6 2.8 %copy-start.1 = (f32[4,2,128,128]{3,2,1,0:T(8,128)}, f32[4,2,128,128]{3,2,1,0:T(8,128)S(1)}, u32[]{:S(2)}) copy-start(f32[4,2,128,128]{3,2,1,0:T(8,128)S(1)} %get-tuple-element.163) | copy-start | bytes 1572868
  138.6 2.8 %copy-start.3 = (f32[128,1024]{1,0:T(8,128)S(1)}, f32[128,1024]{1,0:T(8,128)}, u32[]{:S(2)}) copy-start(f32[128,1024]{1,0:T(8,128)} %copy-done.2) | copy-start | bytes 1572868
  138.6 2.8 %copy-start.5 = (f32[128,1024]{1,0:T(8,128)S(1)}, f32[128,1024]{1,0:T(8,128)}, u32[]{:S(2)}) copy-start(f32[128,1024]{1,0:T(8,128)} %copy-done.4) | copy-start | bytes 1572868
  145.0 19.7 %all-to-all-start.14 = ((bf16[4,4,2,128,128]{3,4,1,2,0:T(8,128)(2,1)}), bf16[4,4,2,128,128]{3,4,1,2,0:T(8,128)(2,1)S(1)}, u32[]{:S(2)}, u32[]{:S(2)}) async-start(bf16[4,4,2,128,128]{3,4,1,2,0:T(8,128)(2,1)} %copy.75), calls=%async_computation.14 | async-start | bytes 2097152 | tf_op jit(solution)/shard_map/all_to_all | solution.py:86

commit v2 on v0

--- a/solution.py
+++ b/solution.py
@@ -130,8 +130,15 @@
     last_sent = split_for_win(lag_terms(first, second, last[None]))
     early_sum = sum_over_win(early_arrived)
     last_sum = sum_over_win(pass_over_win(last_sent))
-    by_rank = jnp.concatenate([early_sum, last_sum], axis=1)
-    return jnp.take(by_rank, rank, axis=1)
+    slots = [
+        jnp.where(
+            rank[k] == K - 1,
+            last_sum[:, 0],
+            lax.dynamic_index_in_dim(early_sum, jnp.minimum(rank[k], K - 2), 1, keepdims=False),
+        )
+        for k in range(K)
+    ]
+    return jnp.stack(slots, axis=1)
 
 
 def solution(mesh):

time: 133 us -> 160 us (1.20)
  the two profiles are of different devices: /device:TPU:216 before, /device:TPU:248 now
where the time goes in v2:
time: 160 us
  waiting for transfers between devices  106 us (66%)
  starting transfers between devices  19.2 us (12%)
  matrix products  16.9 us (11%)
  between operations  7.84 us (5%)
  other arithmetic  5.28 us (3%)
  local copies, waits for them, and re-layouts  4.09 us (3%)
    ppermute x4, waiting for transfers between devices, shifted(): return lambda x: lax.ppermute(x, 'chan', pairs)  84.1 us
    all_to_all x2, waiting for transfers between devices, pass_over_win(): return lax.all_to_all(sent, 'win', split_axis=0, concat_axis=0, tiled=True)  22.1 us
    ppermute x4, starting transfers between devices, shifted(): return lambda x: lax.ppermute(x, 'chan', pairs)  10.4 us
    all_to_all x2, starting transfers between devices, pass_over_win(): return lax.all_to_all(sent, 'win', split_axis=0, concat_axis=0, tiled=True)  8.8 us
    dot_general x2, matrix products, lag_terms(): jnp.einsum('ctf,kjf->tkcj', first, partner[:, 0], preferred_element_type=...  5.76 us
    dot_general x2, matrix products, lag_terms(): jnp.einsum('ctf,kjf->tkcj', second, partner[:, 1], preferred_element_type...  5.23 us
    dot_general x1, matrix products, whiten(): spec = jnp.dot(shaped, table, preferred_element_type=jnp.float32)  4.69 us
  transfers between devices with their start and end apart: 6, of which 5 were waited for; matrix products, arithmetic and copies ran while one was open for 1% of the time, Pallas kernels for 0%

profile of v2, /device:TPU:248, one launch (start us, length us, event | category | flops | bytes accessed | tf_op | source)
XLA Modules:
  0.0 159.9 jit_solution(2043945459174703961)
XLA Ops:
  0.1 0.2 convert_reduce_fusion.14
  1.0 0.7 compare_select_fusion.2
  1.8 0.7 sort.15
  2.6 0.2 constant_dynamic-slice_fusion
  3.0 4.7 %fusion.38 = f32[128,2048]{1,0:T(8,128)S(1)} fusion(bf16[2048,2048]{1,0:T(8,128)(2,1)} %constant.119.clone, bf16[128,2048]{1,0:T(8,128)(2,1)S(1)} %constant_dynamic-slice_fusion, f32[2048]{0:T(1024)S(1)} %multiply_subtract_fusion, f32[128]{0:T(128)S(1)} %broadcast_multiply_fusion), kind=kOutput, calls=%fused_computation.64 | convolution fusion | flops 1074790400 | bytes 9970176 | tf_op jit(solution)/shard_map/dot_general | solution.py:57
  7.7 1.2 fusion.52
  9.0 0.9 pad_maximum_fusion.2
  9.9 1.9 %collective-permute-start.42 = (bf16[2,128,1024]{2,1,0:T(8,128)(2,1)}, bf16[2,128,1024]{2,1,0:T(8,128)(2,1)S(1)}, u32[]{:S(2)}, u32[]{:S(2)}) collective-permute-start(bf16[2,128,1024]{2,1,0:T(8,128)(2,1)} %pad_maximum_fusion.2), channel_id=1, source_target_pairs={{60,0},{64,4},{68,8},{72,12},{76,16},{80,20},{84,24},{88,28},{92,3... | collective-permute-start | bytes 1572872 | tf_op jit(solution)/shard_map/ppermute | solution.py:113
  11.9 0.7 fusion.54
  13.2 35.4 %conditional.3 = (bf16[1,2,128,1024]{3,2,1,0:T(8,128)(2,1)}) conditional(s32[]{:T(128)} %bitcast.34, bf16[2,128,1024]{2,1,0:T(8,128)(2,1)} %pad_maximum_fusion.2, bf16[2,128,1024]{2,1,0:T(8,128)(2,1)} %pad_maximum_fusion.2, bf16[2,128,1024]{2,1,0:T(8,128)(2,1)} %pad_maximum_fusion.2, ...), branch_computations={%region_4.5_spmd, %region_5.6_spmd, %region_6.7_spmd, %region_7.8_... | conditional | bytes 2097200 | solution.py:120
  13.2 3.1 %collective-permute-start.10 = (bf16[2,128,1024]{2,1,0:T(8,128)(2,1)}, bf16[2,128,1024]{2,1,0:T(8,128)(2,1)}, u32[]{:S(2)}, u32[]{:S(2)}) collective-permute-start(bf16[2,128,1024]{2,1,0:T(8,128)(2,1)} %param.10), channel_id=1, source_target_pairs={{44,0},{48,4},{52,8},{56,12},{60,16},{64,20},{68,24},{72,28},{76,3... | collective-permute-start | bytes 1572872 | tf_op jit(solution)/shard_map/cond/branch_10_fun/ppermute | solution.py:113
  16.3 32.3 %collective-permute-done.10 = bf16[2,128,1024]{2,1,0:T(8,128)(2,1)} collective-permute-done((bf16[2,128,1024]{2,1,0:T(8,128)(2,1)}, bf16[2,128,1024]{2,1,0:T(8,128)(2,1)}, u32[]{:S(2)}, u32[]{:S(2)}) %collective-permute-start.10) | collective-permute-done | bytes 524320 | tf_op jit(solution)/shard_map/cond/branch_10_fun/ppermute | solution.py:113
  49.2 43.7 %conditional.4 = (bf16[1,2,128,1024]{3,2,1,0:T(8,128)(2,1)}) conditional(s32[]{:T(128)} %bitcast.35, bf16[2,128,1024]{2,1,0:T(8,128)(2,1)} %pad_maximum_fusion.2, bf16[2,128,1024]{2,1,0:T(8,128)(2,1)} %pad_maximum_fusion.2, bf16[2,128,1024]{2,1,0:T(8,128)(2,1)} %pad_maximum_fusion.2, ...), branch_computations={%region_18.19_spmd, %region_19.20_spmd, %region_20.21_spmd, %regio... | conditional | bytes 2097200 | solution.py:120
  49.2 1.9 %collective-permute-start.23 = (bf16[2,128,1024]{2,1,0:T(8,128)(2,1)}, bf16[2,128,1024]{2,1,0:T(8,128)(2,1)}, u32[]{:S(2)}, u32[]{:S(2)}) collective-permute-start(bf16[2,128,1024]{2,1,0:T(8,128)(2,1)} %param.23), channel_id=1, source_target_pairs={{40,0},{44,4},{48,8},{52,12},{56,16},{60,20},{64,24},{68,28},{72,3... | collective-permute-start | bytes 1572872 | tf_op jit(solution)/shard_map/cond/branch_9_fun/ppermute | solution.py:113
  51.2 41.7 %collective-permute-done.23 = bf16[2,128,1024]{2,1,0:T(8,128)(2,1)} collective-permute-done((bf16[2,128,1024]{2,1,0:T(8,128)(2,1)}, bf16[2,128,1024]{2,1,0:T(8,128)(2,1)}, u32[]{:S(2)}, u32[]{:S(2)}) %collective-permute-start.23) | collective-permute-done | bytes 524320 | tf_op jit(solution)/shard_map/cond/branch_9_fun/ppermute | solution.py:113
  93.5 0.3 cosine_multiply_fusion
  93.9 1.4 pad_maximum_fusion
  95.3 1.9 %fusion.4 = f32[3,128,128,16]{2,1,3,0:T(8,128)S(1)} fusion(f32[16,1024]{1,0:T(8,128)S(1)} %get-tuple-element.259, f32[128,1024]{1,0:T(8,128)S(1)} %get-tuple-element.252, f32[16,1024]{1,0:T(8,128)S(1)} %get-tuple-element.258, f32[128,1024]{1,0:T(8,128)S(1)} %get-tuple-element.248, bf16[3,2,128,1024]{3,2,1,0:T(8,128)(2,1)S(1)} %pad_maximum_fusion), kind=kOutput, calls=%fused_computation.22 | convolution fusion | flops 1619001344 | bytes 5111808 | tf_op jit(solution)/shard_map/ctf,kjf->tkcj/dot_general | solution.py:77
  97.2 2.9 %add_convert_fusion.2 = bf16[3,128,128,16]{2,1,3,0:T(8,128)(2,1)S(1)} fusion(f32[3,128,128,16]{2,1,3,0:T(8,128)S(1)} %fusion.4, f32[16,1024]{1,0:T(8,128)S(1)} %get-tuple-element.259, f32[128,1024]{1,0:T(8,128)} %copy-done.4, f32[16,1024]{1,0:T(8,128)S(1)} %get-tuple-element.258, f32[128,1024]{1,0:T(8,128)S(1)} %get-tuple-element.248, ...), kind=kOutput, calls=%fused_computation.42 | convolution fusion | flops 1620574208 | bytes 6684672 | tf_op jit(solution)/shard_map/ctf,kjf->tkcj/dot_general | solution.py:75
  100.1 37.8 %conditional.5 = (bf16[2,128,1024]{2,1,0:T(8,128)(2,1)}, f32[4,3,128,128]{2,3,0,1:T(8,128)S(1)}) conditional(s32[]{:T(128)} %bitcast.30, (bf16[2,128,1024]{2,1,0:T(8,128)(2,1)}, bf16[4,4,3,128,128]{3,4,1,0,2:T(8,128)(2,1)S(1)}) %tuple.304, (bf16[2,128,1024]{2,1,0:T(8,128)(2,1)}, ...), branch_computations={%region_32.34_spmd, %region_34.36_spmd, %region_36.38_spmd, %regio... | conditional | flops 1376256 | bytes 13893720 | solution.py:127
  100.3 1.6 %copy.47 = bf16[4,4,3,128,128]{4,3,2,1,0:T(8,128)(2,1)} copy(bf16[4,4,3,128,128]{3,4,1,0,2:T(8,128)(2,1)S(1)} %get-tuple-element.234) | data formatting | bytes 3145728 | tf_op jit(solution)/shard_map
  101.9 4.3 %all-to-all-start.7 = ((bf16[4,4,3,128,128]{4,3,2,1,0:T(8,128)(2,1)}), bf16[4,4,3,128,128]{4,3,2,1,0:T(8,128)(2,1)S(1)}, u32[]{:S(2)}, u32[]{:S(2)}) async-start(bf16[4,4,3,128,128]{4,3,2,1,0:T(8,128)(2,1)} %copy.47), calls=%async_computation.7 | async-start | bytes 3145728 | tf_op jit(solution)/shard_map/cond/branch_7_fun/all_to_all | solution.py:86
  106.2 3.5 %collective-permute-start.35 = (bf16[2,128,1024]{2,1,0:T(8,128)(2,1)}, bf16[2,128,1024]{2,1,0:T(8,128)(2,1)}, u32[]{:S(2)}, u32[]{:S(2)}) collective-permute-start(bf16[2,128,1024]{2,1,0:T(8,128)(2,1)} %get-tuple-element.137), channel_id=1, source_target_pairs={{32,0},{36,4},{40,8},{44,12},{48,16},{52,20},{56,24},{60,28},{64,3... | collective-permute-start | bytes 1572872 | tf_op jit(solution)/shard_map/cond/branch_7_fun/ppermute | solution.py:113
  109.7 17.4 %all-to-all-done.7 = bf16[4,4,3,128,128]{4,3,2,1,0:T(8,128)(2,1)S(1)} async-done(((bf16[4,4,3,128,128]{4,3,2,1,0:T(8,128)(2,1)}), bf16[4,4,3,128,128]{4,3,2,1,0:T(8,128)(2,1)S(1)}, u32[]{:S(2)}, u32[]{:S(2)}) %all-to-all-start.7) | async-done | bytes 1572896 | tf_op jit(solution)/shard_map/cond/branch_7_fun/all_to_all | solution.py:86
  127.2 0.3 convert_reduce_fusion.7
  127.4 0.3 copy.70
  127.7 10.2 %collective-permute-done.35 = bf16[2,128,1024]{2,1,0:T(8,128)(2,1)} collective-permute-done((bf16[2,128,1024]{2,1,0:T(8,128)(2,1)}, bf16[2,128,1024]{2,1,0:T(8,128)(2,1)}, u32[]{:S(2)}, u32[]{:S(2)}) %collective-permute-start.35) | collective-permute-done | bytes 524320 | tf_op jit(solution)/shard_map/cond/branch_7_fun/ppermute | solution.py:113
  137.9 2.9 %fusion = f32[128,128,16]{1,0,2:T(8,128)S(1)} fusion(f32[16,1024]{1,0:T(8,128)S(1)} %get-tuple-element.259, f32[128,1024]{1,0:T(8,128)} %copy-done.4, f32[16,1024]{1,0:T(8,128)S(1)} %get-tuple-element.258, f32[128,1024]{1,0:T(8,128)} %copy-done.2, bf16[1,2,128,1024]{3,2,1,0:T(8,128)(2,1)} %bitcast.46), kind=kOutput, calls=%fused_computation.18 | convolution fusion | flops 545259520 | bytes 2490368 | tf_op jit(solution)/shard_map/ctf,kjf->tkcj/dot_general | solution.py:75
  140.8 3.4 %fusion.30 = bf16[128,128,16]{1,0,2:T(8,128)(2,1)} fusion(f32[128,128,16]{1,0,2:T(8,128)S(1)} %fusion, f32[16,1024]{1,0:T(8,128)S(1)} %get-tuple-element.259, f32[128,1024]{1,0:T(8,128)S(1)} %copy-done.5, f32[16,1024]{1,0:T(8,128)S(1)} %get-tuple-element.258, f32[128,1024]{1,0:T(8,128)S(1)} %copy-done.3, bf16[1,2,128,1024]{3,2,1,0:T(8,128)(2,1)} %bitcast.46), kind=kOutput, calls=%fused_computation.49 | convolution fusion | flops 545783808 | bytes 3014656 | tf_op jit(solution)/shard_map/ctf,kjf->tkcj/dot_general | solution.py:77
  144.1 4.5 %all-to-all-start.14 = ((bf16[4,4,1,128,128]{3,4,1,2,0:T(8,128)(2,1)}), bf16[4,4,1,128,128]{3,4,1,2,0:T(8,128)(2,1)S(1)}, u32[]{:S(2)}, u32[]{:S(2)}) async-start(bf16[4,4,1,128,128]{3,4,1,2,0:T(8,128)(2,1)} %bitcast.54), calls=%async_computation.14 | async-start | bytes 1048576 | tf_op jit(solution)/shard_map/all_to_all | solution.py:86
  153.7 4.6 %all-to-all-done.14 = bf16[4,4,1,128,128]{3,4,1,2,0:T(8,128)(2,1)S(1)} async-done(((bf16[4,4,1,128,128]{3,4,1,2,0:T(8,128)(2,1)}), bf16[4,4,1,128,128]{3,4,1,2,0:T(8,128)(2,1)S(1)}, u32[]{:S(2)}, u32[]{:S(2)}) %all-to-all-start.14) | async-done | bytes 524320 | tf_op jit(solution)/shard_map/all_to_all | solution.py:86
  158.6 1.3 copy.60
  (24 shorter events, 0.8 us)
Async XLA Ops:
  0.0 2.6 %copy-start = (bf16[128,4096]{1,0:T(8,128)(2,1)S(1)}, bf16[128,4096]{1,0:T(8,128)(2,1)}, u32[]{:S(2)}) copy-start(bf16[128,4096]{1,0:T(8,128)(2,1)} %param.46) | copy-start | bytes 3145732
  9.0 86.3 %copy-start.4 = (f32[128,1024]{1,0:T(8,128)}, f32[128,1024]{1,0:T(8,128)S(1)}, u32[]{:S(2)}) copy-start(f32[128,1024]{1,0:T(8,128)S(1)} %get-tuple-element.252) | copy-start | bytes 1572868
  9.0 88.2 %copy-start.2 = (f32[128,1024]{1,0:T(8,128)}, f32[128,1024]{1,0:T(8,128)S(1)}, u32[]{:S(2)}) copy-start(f32[128,1024]{1,0:T(8,128)S(1)} %get-tuple-element.248) | copy-start | bytes 1572868
  9.9 84.0 %collective-permute-start.42 = (bf16[2,128,1024]{2,1,0:T(8,128)(2,1)}, bf16[2,128,1024]{2,1,0:T(8,128)(2,1)S(1)}, u32[]{:S(2)}, u32[]{:S(2)}) collective-permute-start(bf16[2,128,1024]{2,1,0:T(8,128)(2,1)} %pad_maximum_fusion.2), channel_id=1, source_target_pairs={{60,0},{64,4},{68,8},{72,12},{76,16},{80,20},{84,24},{88,28},{92,3... | collective-permute-start | bytes 1572872 | tf_op jit(solution)/shard_map/ppermute | solution.py:113
  13.2 35.3 %collective-permute-start.10 = (bf16[2,128,1024]{2,1,0:T(8,128)(2,1)}, bf16[2,128,1024]{2,1,0:T(8,128)(2,1)}, u32[]{:S(2)}, u32[]{:S(2)}) collective-permute-start(bf16[2,128,1024]{2,1,0:T(8,128)(2,1)} %param.10), channel_id=1, source_target_pairs={{44,0},{48,4},{52,8},{56,12},{60,16},{64,20},{68,24},{72,28},{76,3... | collective-permute-start | bytes 1572872 | tf_op jit(solution)/shard_map/cond/branch_10_fun/ppermute | solution.py:113
  49.2 43.6 %collective-permute-start.23 = (bf16[2,128,1024]{2,1,0:T(8,128)(2,1)}, bf16[2,128,1024]{2,1,0:T(8,128)(2,1)}, u32[]{:S(2)}, u32[]{:S(2)}) collective-permute-start(bf16[2,128,1024]{2,1,0:T(8,128)(2,1)} %param.23), channel_id=1, source_target_pairs={{40,0},{44,4},{48,8},{52,12},{56,16},{60,20},{64,24},{68,28},{72,3... | collective-permute-start | bytes 1572872 | tf_op jit(solution)/shard_map/cond/branch_9_fun/ppermute | solution.py:113
  101.9 25.2 %all-to-all-start.7 = ((bf16[4,4,3,128,128]{4,3,2,1,0:T(8,128)(2,1)}), bf16[4,4,3,128,128]{4,3,2,1,0:T(8,128)(2,1)S(1)}, u32[]{:S(2)}, u32[]{:S(2)}) async-start(bf16[4,4,3,128,128]{4,3,2,1,0:T(8,128)(2,1)} %copy.47), calls=%async_computation.7 | async-start | bytes 3145728 | tf_op jit(solution)/shard_map/cond/branch_7_fun/all_to_all | solution.py:86
  106.2 31.6 %collective-permute-start.35 = (bf16[2,128,1024]{2,1,0:T(8,128)(2,1)}, bf16[2,128,1024]{2,1,0:T(8,128)(2,1)}, u32[]{:S(2)}, u32[]{:S(2)}) collective-permute-start(bf16[2,128,1024]{2,1,0:T(8,128)(2,1)} %get-tuple-element.137), channel_id=1, source_target_pairs={{32,0},{36,4},{40,8},{44,12},{48,16},{52,20},{56,24},{60,28},{64,3... | collective-permute-start | bytes 1572872 | tf_op jit(solution)/shard_map/cond/branch_7_fun/ppermute | solution.py:113
  137.9 2.9 %copy-start.3 = (f32[128,1024]{1,0:T(8,128)S(1)}, f32[128,1024]{1,0:T(8,128)}, u32[]{:S(2)}) copy-start(f32[128,1024]{1,0:T(8,128)} %copy-done.2) | copy-start | bytes 1572868
  137.9 2.9 %copy-start.5 = (f32[128,1024]{1,0:T(8,128)S(1)}, f32[128,1024]{1,0:T(8,128)}, u32[]{:S(2)}) copy-start(f32[128,1024]{1,0:T(8,128)} %copy-done.4) | copy-start | bytes 1572868
  144.1 14.2 %all-to-all-start.14 = ((bf16[4,4,1,128,128]{3,4,1,2,0:T(8,128)(2,1)}), bf16[4,4,1,128,128]{3,4,1,2,0:T(8,128)(2,1)S(1)}, u32[]{:S(2)}, u32[]{:S(2)}) async-start(bf16[4,4,1,128,128]{3,4,1,2,0:T(8,128)(2,1)} %bitcast.54), calls=%async_computation.14 | async-start | bytes 1048576 | tf_op jit(solution)/shard_map/all_to_all | solution.py:86
  158.4 1.5 copy-start.1

commit v3 on v2

--- a/solution.py
+++ b/solution.py
@@ -117,7 +117,7 @@
     moves = [shifted(by) for by in range(1, far)]
     cos_w, sin_w = phase_tables(groups)
     first, second = lag_factors(own_re, own_im, cos_w, sin_w)
-    nearer = [lax.switch(order[k] - 1, moves, spectra) for k in range(K - 2)]
+    nearer = [lax.switch(order[k] - 1, moves, spectra) for k in (0, K - 2)]
     early = jnp.stack([farthest] + nearer, axis=0)
     early_sent = lax.optimization_barrier(split_for_win(lag_terms(first, second, early)))
 
@@ -125,16 +125,17 @@
         return lambda x, sent: (move(x), pass_over_win(sent))
 
     last, early_arrived = lax.switch(
-        order[K - 2] - 1, [with_early(move) for move in moves], spectra, early_sent
+        order[1] - 1, [with_early(move) for move in moves], spectra, early_sent
     )
     last_sent = split_for_win(lag_terms(first, second, last[None]))
     early_sum = sum_over_win(early_arrived)
     last_sum = sum_over_win(pass_over_win(last_sent))
+    place = jnp.array([0, 1, 3, 2], jnp.int32)[rank]
     slots = [
         jnp.where(
-            rank[k] == K - 1,
+            place[k] == K - 1,
             last_sum[:, 0],
-            lax.dynamic_index_in_dim(early_sum, jnp.minimum(rank[k], K - 2), 1, keepdims=False),
+            lax.dynamic_index_in_dim(early_sum, jnp.minimum(place[k], K - 2), 1, keepdims=False),
         )
         for k in range(K)
     ]

time: 160 us -> 136 us (0.85)
  waiting for transfers between devices: 106 us -> 79.2 us
    ppermute x4, waiting for transfers between devices: 84.1 us -> 59.4 us  [shifted(): return lambda x: lax.ppermute(x, 'chan', pairs)]
    all_to_all x2, waiting for transfers between devices: 22.1 us -> 19.7 us  [pass_over_win(): return lax.all_to_all(sent, 'win', split_axis=0, concat_axis=0, tiled=True)]
  transfers between devices with their start and end apart: 6 -> 6, of which waited for: 5 -> 5; matrix products, arithmetic and copies ran while one was open for 1% -> 2% of each run, Pallas kernels for 0% -> 0%
where the time goes in v3:
time: 136 us; the launch traced here: 135 us
  waiting for transfers between devices  79.2 us (58%)
  starting transfers between devices  20.4 us (15%)
  matrix products  16.9 us (12%)
  between operations  7.6 us (6%)
  other arithmetic  5.34 us (4%)
  local copies, waits for them, and re-layouts  5.32 us (4%)
    ppermute x4, waiting for transfers between devices, shifted(): return lambda x: lax.ppermute(x, 'chan', pairs)  59.4 us
    all_to_all x2, waiting for transfers between devices, pass_over_win(): return lax.all_to_all(sent, 'win', split_axis=0, concat_axis=0, tiled=True)  19.7 us
    ppermute x4, starting transfers between devices, shifted(): return lambda x: lax.ppermute(x, 'chan', pairs)  11.9 us
    all_to_all x2, starting transfers between devices, pass_over_win(): return lax.all_to_all(sent, 'win', split_axis=0, concat_axis=0, tiled=True)  8.49 us
    dot_general x2, matrix products, lag_terms(): jnp.einsum('ctf,kjf->tkcj', first, partner[:, 0], preferred_element_type=...  5.76 us
    dot_general x2, matrix products, lag_terms(): jnp.einsum('ctf,kjf->tkcj', second, partner[:, 1], preferred_element_type...  5.21 us
    dot_general x1, matrix products, whiten(): spec = jnp.dot(shaped, table, preferred_element_type=jnp.float32)  4.7 us
  transfers between devices with their start and end apart: 6, of which 5 were waited for; matrix products, arithmetic and copies ran while one was open for 2% of the time, Pallas kernels for 0%

profile of v3, /device:TPU:248, one launch (start us, length us, event | category | flops | bytes accessed | tf_op | source)
XLA Modules:
  0.0 135.1 jit_solution(7161302370436777881)
XLA Ops:
  1.0 0.7 compare_select_fusion.3
  1.8 0.8 sort.15
  3.1 4.7 %fusion.38 = f32[128,2048]{1,0:T(8,128)S(1)} fusion(bf16[2048,2048]{1,0:T(8,128)(2,1)} %constant.124.clone, bf16[128,2048]{1,0:T(8,128)(2,1)S(1)} %constant_dynamic-slice_fusion, f32[2048]{0:T(1024)S(1)} %multiply_subtract_fusion, f32[128]{0:T(128)S(1)} %broadcast_multiply_fusion), kind=kOutput, calls=%fused_computation.65 | convolution fusion | flops 1074790400 | bytes 9970176 | tf_op jit(solution)/shard_map/dot_general | solution.py:57
  7.8 1.2 fusion.52
  9.1 0.9 pad_maximum_fusion.2
  10.0 1.9 %collective-permute-start.42 = (bf16[2,128,1024]{2,1,0:T(8,128)(2,1)}, bf16[2,128,1024]{2,1,0:T(8,128)(2,1)S(1)}, u32[]{:S(2)}, u32[]{:S(2)}) collective-permute-start(bf16[2,128,1024]{2,1,0:T(8,128)(2,1)} %pad_maximum_fusion.2), channel_id=1, source_target_pairs={{60,0},{64,4},{68,8},{72,12},{76,16},{80,20},{84,24},{88,28},{92,3... | collective-permute-start | bytes 1572872 | tf_op jit(solution)/shard_map/ppermute | solution.py:113
  11.9 0.6 fusion.55
  13.7 33.4 %conditional.4 = (bf16[1,2,128,1024]{3,2,1,0:T(8,128)(2,1)}) conditional(s32[]{:T(128)} %bitcast.35, bf16[2,128,1024]{2,1,0:T(8,128)(2,1)} %pad_maximum_fusion.2, bf16[2,128,1024]{2,1,0:T(8,128)(2,1)} %pad_maximum_fusion.2, bf16[2,128,1024]{2,1,0:T(8,128)(2,1)} %pad_maximum_fusion.2, ...), branch_computations={%region_18.19_spmd, %region_19.20_spmd, %region_20.21_spmd, %regio... | conditional | bytes 2097200 | solution.py:120
  13.8 4.7 %collective-permute-start.21 = (bf16[2,128,1024]{2,1,0:T(8,128)(2,1)}, bf16[2,128,1024]{2,1,0:T(8,128)(2,1)}, u32[]{:S(2)}, u32[]{:S(2)}) collective-permute-start(bf16[2,128,1024]{2,1,0:T(8,128)(2,1)} %param.21), channel_id=1, source_target_pairs={{32,0},{36,4},{40,8},{44,12},{48,16},{52,20},{56,24},{60,28},{64,3... | collective-permute-start | bytes 1572872 | tf_op jit(solution)/shard_map/cond/branch_7_fun/ppermute | solution.py:113
  18.5 28.7 %collective-permute-done.21 = bf16[2,128,1024]{2,1,0:T(8,128)(2,1)} collective-permute-done((bf16[2,128,1024]{2,1,0:T(8,128)(2,1)}, bf16[2,128,1024]{2,1,0:T(8,128)(2,1)}, u32[]{:S(2)}, u32[]{:S(2)}) %collective-permute-start.21) | collective-permute-done | bytes 524320 | tf_op jit(solution)/shard_map/cond/branch_7_fun/ppermute | solution.py:113
  47.8 17.0 %conditional.3 = (bf16[1,2,128,1024]{3,2,1,0:T(8,128)(2,1)}) conditional(s32[]{:T(128)} %bitcast.34, bf16[2,128,1024]{2,1,0:T(8,128)(2,1)} %pad_maximum_fusion.2, bf16[2,128,1024]{2,1,0:T(8,128)(2,1)} %pad_maximum_fusion.2, bf16[2,128,1024]{2,1,0:T(8,128)(2,1)} %pad_maximum_fusion.2, ...), branch_computations={%region_4.5_spmd, %region_5.6_spmd, %region_6.7_spmd, %region_7.8_... | conditional | bytes 2097200 | solution.py:120
  47.8 1.9 %collective-permute-start.13 = (bf16[2,128,1024]{2,1,0:T(8,128)(2,1)}, bf16[2,128,1024]{2,1,0:T(8,128)(2,1)}, u32[]{:S(2)}, u32[]{:S(2)}) collective-permute-start(bf16[2,128,1024]{2,1,0:T(8,128)(2,1)} %param.13), channel_id=1, source_target_pairs={{56,0},{60,4},{64,8},{68,12},{72,16},{76,20},{80,24},{84,28},{88,3... | collective-permute-start | bytes 1572872 | tf_op jit(solution)/shard_map/cond/branch_13_fun/ppermute | solution.py:113
  49.8 15.1 %collective-permute-done.13 = bf16[2,128,1024]{2,1,0:T(8,128)(2,1)} collective-permute-done((bf16[2,128,1024]{2,1,0:T(8,128)(2,1)}, bf16[2,128,1024]{2,1,0:T(8,128)(2,1)}, u32[]{:S(2)}, u32[]{:S(2)}) %collective-permute-start.13) | collective-permute-done | bytes 524320 | tf_op jit(solution)/shard_map/cond/branch_13_fun/ppermute | solution.py:113
  64.8 0.3 cosine_multiply_fusion
  65.2 1.4 %pad_maximum_fusion = bf16[3,2,128,1024]{3,2,1,0:T(8,128)(2,1)S(1)} fusion(bf16[1,2,128,1024]{3,2,1,0:T(8,128)(2,1)} %get-tuple-element.324, bf16[1,2,128,1024]{3,2,1,0:T(8,128)(2,1)} %get-tuple-element.323, bf16[1,2,128,1024]{3,2,1,0:T(8,128)(2,1)S(1)} %bitcast.110), kind=kLoop, calls=%fused_computation.46 | loop fusion | flops 1572864 | bytes 3145728 | tf_op jit(solution)/shard_map/stack | solution.py:121
  66.6 1.9 %fusion.4 = f32[3,128,128,16]{2,1,3,0:T(8,128)S(1)} fusion(f32[16,1024]{1,0:T(8,128)S(1)} %get-tuple-element.287, f32[128,1024]{1,0:T(8,128)S(1)} %get-tuple-element.280, f32[16,1024]{1,0:T(8,128)S(1)} %get-tuple-element.286, f32[128,1024]{1,0:T(8,128)S(1)} %get-tuple-element.276, bf16[3,2,128,1024]{3,2,1,0:T(8,128)(2,1)S(1)} %pad_maximum_fusion), kind=kOutput, calls=%fused_computation.23 | convolution fusion | flops 1619001344 | bytes 5111808 | tf_op jit(solution)/shard_map/ctf,kjf->tkcj/dot_general | solution.py:77
  68.5 2.9 %add_convert_fusion.2 = bf16[3,128,128,16]{2,1,3,0:T(8,128)(2,1)S(1)} fusion(f32[3,128,128,16]{2,1,3,0:T(8,128)S(1)} %fusion.4, f32[16,1024]{1,0:T(8,128)S(1)} %get-tuple-element.287, f32[128,1024]{1,0:T(8,128)} %copy-done.5, f32[16,1024]{1,0:T(8,128)S(1)} %get-tuple-element.286, f32[128,1024]{1,0:T(8,128)S(1)} %get-tuple-element.276, ...), kind=kOutput, calls=%fused_computation.43 | convolution fusion | flops 1620574208 | bytes 6684672 | tf_op jit(solution)/shard_map/ctf,kjf->tkcj/dot_general | solution.py:75
  71.4 41.3 %conditional.5 = (bf16[2,128,1024]{2,1,0:T(8,128)(2,1)}, f32[4,3,128,128]{2,3,0,1:T(8,128)S(1)}) conditional(s32[]{:T(128)} %bitcast.30, (bf16[2,128,1024]{2,1,0:T(8,128)(2,1)}, bf16[4,4,3,128,128]{3,4,1,0,2:T(8,128)(2,1)S(1)}) %tuple.315, (bf16[2,128,1024]{2,1,0:T(8,128)(2,1)}, ...), branch_computations={%region_32.34_spmd, %region_34.36_spmd, %region_36.38_spmd, %regio... | conditional | flops 1376256 | bytes 13893720 | solution.py:127
  71.6 1.6 %copy.61 = bf16[4,4,3,128,128]{4,3,2,1,0:T(8,128)(2,1)} copy(bf16[4,4,3,128,128]{3,4,1,0,2:T(8,128)(2,1)S(1)} %get-tuple-element.260) | data formatting | bytes 3145728 | tf_op jit(solution)/shard_map
  73.2 4.2 %all-to-all-start.6 = ((bf16[4,4,3,128,128]{4,3,2,1,0:T(8,128)(2,1)}), bf16[4,4,3,128,128]{4,3,2,1,0:T(8,128)(2,1)S(1)}, u32[]{:S(2)}, u32[]{:S(2)}) async-start(bf16[4,4,3,128,128]{4,3,2,1,0:T(8,128)(2,1)} %copy.61), calls=%async_computation.6 | async-start | bytes 3145728 | tf_op jit(solution)/shard_map/cond/branch_6_fun/all_to_all | solution.py:86
  77.4 3.4 %collective-permute-start.34 = (bf16[2,128,1024]{2,1,0:T(8,128)(2,1)}, bf16[2,128,1024]{2,1,0:T(8,128)(2,1)}, u32[]{:S(2)}, u32[]{:S(2)}) collective-permute-start(bf16[2,128,1024]{2,1,0:T(8,128)(2,1)} %get-tuple-element.135), channel_id=1, source_target_pairs={{28,0},{32,4},{36,8},{40,12},{44,16},{48,20},{52,24},{56,28},{60,3... | collective-permute-start | bytes 1572872 | tf_op jit(solution)/shard_map/cond/branch_6_fun/ppermute | solution.py:113
  80.8 15.6 %all-to-all-done.6 = bf16[4,4,3,128,128]{4,3,2,1,0:T(8,128)(2,1)S(1)} async-done(((bf16[4,4,3,128,128]{4,3,2,1,0:T(8,128)(2,1)}), bf16[4,4,3,128,128]{4,3,2,1,0:T(8,128)(2,1)S(1)}, u32[]{:S(2)}, u32[]{:S(2)}) %all-to-all-start.6) | async-done | bytes 1572896 | tf_op jit(solution)/shard_map/cond/branch_6_fun/all_to_all | solution.py:86
  96.4 0.3 convert_reduce_fusion.6
  96.7 0.3 copy.84
  96.9 15.7 %collective-permute-done.34 = bf16[2,128,1024]{2,1,0:T(8,128)(2,1)} collective-permute-done((bf16[2,128,1024]{2,1,0:T(8,128)(2,1)}, bf16[2,128,1024]{2,1,0:T(8,128)(2,1)}, u32[]{:S(2)}, u32[]{:S(2)}) %collective-permute-start.34) | collective-permute-done | bytes 524320 | tf_op jit(solution)/shard_map/cond/branch_6_fun/ppermute | solution.py:113
  112.6 2.9 %fusion = f32[128,128,16]{1,0,2:T(8,128)S(1)} fusion(f32[16,1024]{1,0:T(8,128)S(1)} %get-tuple-element.287, f32[128,1024]{1,0:T(8,128)} %copy-done.5, f32[16,1024]{1,0:T(8,128)S(1)} %get-tuple-element.286, f32[128,1024]{1,0:T(8,128)} %copy-done.3, bf16[1,2,128,1024]{3,2,1,0:T(8,128)(2,1)} %bitcast.46), kind=kOutput, calls=%fused_computation.19 | convolution fusion | flops 545259520 | bytes 2490368 | tf_op jit(solution)/shard_map/ctf,kjf->tkcj/dot_general | solution.py:75
  115.5 3.3 %fusion.30 = bf16[128,128,16]{1,0,2:T(8,128)(2,1)} fusion(f32[128,128,16]{1,0,2:T(8,128)S(1)} %fusion, f32[16,1024]{1,0:T(8,128)S(1)} %get-tuple-element.287, f32[128,1024]{1,0:T(8,128)S(1)} %copy-done.6, f32[16,1024]{1,0:T(8,128)S(1)} %get-tuple-element.286, f32[128,1024]{1,0:T(8,128)S(1)} %copy-done.4, bf16[1,2,128,1024]{3,2,1,0:T(8,128)(2,1)} %bitcast.46), kind=kOutput, calls=%fused_computation.50 | convolution fusion | flops 545783808 | bytes 3014656 | tf_op jit(solution)/shard_map/ctf,kjf->tkcj/dot_general | solution.py:77
  118.9 4.3 %all-to-all-start.14 = ((bf16[4,4,1,128,128]{3,4,1,2,0:T(8,128)(2,1)}), bf16[4,4,1,128,128]{3,4,1,2,0:T(8,128)(2,1)S(1)}, u32[]{:S(2)}, u32[]{:S(2)}) async-start(bf16[4,4,1,128,128]{3,4,1,2,0:T(8,128)(2,1)} %bitcast.54), calls=%async_computation.14 | async-start | bytes 1048576 | tf_op jit(solution)/shard_map/all_to_all | solution.py:86
  123.2 0.6 gather_fusion
  123.9 0.7 fusion.54
  129.4 4.1 %all-to-all-done.14 = bf16[4,4,1,128,128]{3,4,1,2,0:T(8,128)(2,1)S(1)} async-done(((bf16[4,4,1,128,128]{3,4,1,2,0:T(8,128)(2,1)}), bf16[4,4,1,128,128]{3,4,1,2,0:T(8,128)(2,1)S(1)}, u32[]{:S(2)}, u32[]{:S(2)}) %all-to-all-start.14) | async-done | bytes 524320 | tf_op jit(solution)/shard_map/all_to_all | solution.py:86
  133.8 1.3 copy.75
  (30 shorter events, 1.2 us)
Async XLA Ops:
  0.0 2.7 %copy-start = (bf16[128,4096]{1,0:T(8,128)(2,1)S(1)}, bf16[128,4096]{1,0:T(8,128)(2,1)}, u32[]{:S(2)}) copy-start(bf16[128,4096]{1,0:T(8,128)(2,1)} %param.47) | copy-start | bytes 3145732
  9.0 57.5 %copy-start.5 = (f32[128,1024]{1,0:T(8,128)}, f32[128,1024]{1,0:T(8,128)S(1)}, u32[]{:S(2)}) copy-start(f32[128,1024]{1,0:T(8,128)S(1)} %get-tuple-element.280) | copy-start | bytes 1572868
  9.1 59.4 %copy-start.3 = (f32[128,1024]{1,0:T(8,128)}, f32[128,1024]{1,0:T(8,128)S(1)}, u32[]{:S(2)}) copy-start(f32[128,1024]{1,0:T(8,128)S(1)} %get-tuple-element.276) | copy-start | bytes 1572868
  10.0 55.2 %collective-permute-start.42 = (bf16[2,128,1024]{2,1,0:T(8,128)(2,1)}, bf16[2,128,1024]{2,1,0:T(8,128)(2,1)S(1)}, u32[]{:S(2)}, u32[]{:S(2)}) collective-permute-start(bf16[2,128,1024]{2,1,0:T(8,128)(2,1)} %pad_maximum_fusion.2), channel_id=1, source_target_pairs={{60,0},{64,4},{68,8},{72,12},{76,16},{80,20},{84,24},{88,28},{92,3... | collective-permute-start | bytes 1572872 | tf_op jit(solution)/shard_map/ppermute | solution.py:113
  13.8 33.4 %collective-permute-start.21 = (bf16[2,128,1024]{2,1,0:T(8,128)(2,1)}, bf16[2,128,1024]{2,1,0:T(8,128)(2,1)}, u32[]{:S(2)}, u32[]{:S(2)}) collective-permute-start(bf16[2,128,1024]{2,1,0:T(8,128)(2,1)} %param.21), channel_id=1, source_target_pairs={{32,0},{36,4},{40,8},{44,12},{48,16},{52,20},{56,24},{60,28},{64,3... | collective-permute-start | bytes 1572872 | tf_op jit(solution)/shard_map/cond/branch_7_fun/ppermute | solution.py:113
  47.8 17.0 %collective-permute-start.13 = (bf16[2,128,1024]{2,1,0:T(8,128)(2,1)}, bf16[2,128,1024]{2,1,0:T(8,128)(2,1)}, u32[]{:S(2)}, u32[]{:S(2)}) collective-permute-start(bf16[2,128,1024]{2,1,0:T(8,128)(2,1)} %param.13), channel_id=1, source_target_pairs={{56,0},{60,4},{64,8},{68,12},{72,16},{76,20},{80,24},{84,28},{88,3... | collective-permute-start | bytes 1572872 | tf_op jit(solution)/shard_map/cond/branch_13_fun/ppermute | solution.py:113
  73.2 23.2 %all-to-all-start.6 = ((bf16[4,4,3,128,128]{4,3,2,1,0:T(8,128)(2,1)}), bf16[4,4,3,128,128]{4,3,2,1,0:T(8,128)(2,1)S(1)}, u32[]{:S(2)}, u32[]{:S(2)}) async-start(bf16[4,4,3,128,128]{4,3,2,1,0:T(8,128)(2,1)} %copy.61), calls=%async_computation.6 | async-start | bytes 3145728 | tf_op jit(solution)/shard_map/cond/branch_6_fun/all_to_all | solution.py:86
  77.4 35.2 %collective-permute-start.34 = (bf16[2,128,1024]{2,1,0:T(8,128)(2,1)}, bf16[2,128,1024]{2,1,0:T(8,128)(2,1)}, u32[]{:S(2)}, u32[]{:S(2)}) collective-permute-start(bf16[2,128,1024]{2,1,0:T(8,128)(2,1)} %get-tuple-element.135), channel_id=1, source_target_pairs={{28,0},{32,4},{36,8},{40,12},{44,16},{48,20},{52,24},{56,28},{60,3... | collective-permute-start | bytes 1572872 | tf_op jit(solution)/shard_map/cond/branch_6_fun/ppermute | solution.py:113
  112.6 2.9 %copy-start.4 = (f32[128,1024]{1,0:T(8,128)S(1)}, f32[128,1024]{1,0:T(8,128)}, u32[]{:S(2)}) copy-start(f32[128,1024]{1,0:T(8,128)} %copy-done.3) | copy-start | bytes 1572868
  112.6 2.9 %copy-start.6 = (f32[128,1024]{1,0:T(8,128)S(1)}, f32[128,1024]{1,0:T(8,128)}, u32[]{:S(2)}) copy-start(f32[128,1024]{1,0:T(8,128)} %copy-done.5) | copy-start | bytes 1572868
  115.5 7.7 %copy-start.2 = (s32[4]{0:T(128)S(1)}, s32[4]{0:T(128)}, u32[]{:S(2)}) copy-start(s32[4]{0:T(128)} %constant.125.clone) | copy-start | bytes 52
  118.9 14.6 %all-to-all-start.14 = ((bf16[4,4,1,128,128]{3,4,1,2,0:T(8,128)(2,1)}), bf16[4,4,1,128,128]{3,4,1,2,0:T(8,128)(2,1)S(1)}, u32[]{:S(2)}, u32[]{:S(2)}) async-start(bf16[4,4,1,128,128]{3,4,1,2,0:T(8,128)(2,1)} %bitcast.54), calls=%async_computation.14 | async-start | bytes 1048576 | tf_op jit(solution)/shard_map/all_to_all | solution.py:86
  133.6 1.5 %copy-start.1 = (bf16[128,4096]{1,0:T(8,128)(2,1)S(1)}, bf16[128,4096]{1,0:T(8,128)(2,1)}, u32[]{:S(2)}) copy-start(bf16[128,4096]{1,0:T(8,128)(2,1)} %param.47) | copy-start | bytes 3145732
